TPU v7x, 512 devices: a whole 4x4x16 slice. The times are simulated.
512 devices in a mesh: sub: 128 (over y, z, core), case: 4 (over x).
Axes of the slice: x: 4, y: 4, z: 16, core: 2. Of those that a mesh axis runs over, the one named last changes fastest.
Arguments:
- load_interior: float32 [128, 128, 4096], P('sub', None, 'case'), may hold values from -6 to 6
- load_boundary: float32 [128, 128, 1024], P('sub', None, 'case'), may hold values from -6 to 6
- cond_blocks: float32 [128, 128, 4096], P('sub', 'case'), may hold values from -0.25 to 0.25
- block_rows: int32 [128, 128], P('sub', 'case'), may hold values from 0 to 15
- block_cols: int32 [128, 128], P('sub', 'case'), may hold values from 0 to 63, as said below
- interface_maps: int32 [128, 7, 2, 1024], P('sub'), may hold values from 0 to 1023, as said below
- merge_maps: float32 [128, 7, 1024, 512], P('sub', None, 'case'), as said below
Outputs:
- leaf_loads: float32 [128, 1024, 128], P('sub', 'case')
- node_loads: float32 [128, 1024, 128], P('sub', 'case')
Inputs may be any that keep to these rules, and one draw needn't show every extreme that they name: `block_cols`: entry k of a substructure's row lies in [(k // 32) * 16, (k // 32 + 1) * 16); blocks may repeat. `interface_maps`: each row of 1024 entries is a permutation; at level index l, slots that agree in all but their lowest l + 1 bits hold equal entries. `merge_maps`: at level index l, slots that agree in all but their lowest l + 1 bits hold equal entries.
All inputs are finite; a program needn't handle non-finite values.
Results may differ from a plain program's by a relative error of at most 0.0003.
Values sent between devices are 32-bit elements; how exact they have to be, the bound alone decides.
No kernel may reach another device: no remote copies, remote signals or barrier semaphores. Data moves between devices by JAX's collectives and lax.ppermute only.
A program may use at most 64 MiB of HBM per device.

v0:
```python
import jax
import jax.numpy as jnp
from jax import lax
from jax.sharding import PartitionSpec as P

BLK = 64


def from_partner(value, axis, distance):
    mask = 2**distance
    pairs = [(source, source ^ mask) for source in range(lax.axis_size(axis))]
    return lax.ppermute(value, axis, pairs)


def on_device(
    load_interior, load_boundary, cond_blocks, block_rows, block_cols, interface_maps, merge_maps
):
    interior, boundary = (
        lax.all_to_all(load_interior, "sub", split_axis=1, concat_axis=0, tiled=True),
        lax.all_to_all(load_boundary, "sub", split_axis=1, concat_axis=0, tiled=True),
    )
    interior = jnp.transpose(interior[:, 0, :])
    boundary = jnp.transpose(boundary[:, 0, :])
    local_rows = interior.shape[0]
    num_cases = interior.shape[1]
    block_count = cond_blocks.shape[1]
    block_size = BLK
    blocks = cond_blocks[0].reshape(block_count, block_size, block_size)
    quarter = boundary.shape[0]
    groups = lax.axis_size("case")
    full_rows = quarter * groups
    position = lax.axis_index("case")
    local_cols = block_cols[0] - position * (local_rows // block_size)
    pieces = jnp.take(
        interior.reshape(local_rows // block_size, block_size, num_cases), local_cols, axis=0
    )
    products = jnp.einsum("krc,kcn->krn", blocks, pieces, precision=lax.Precision.HIGHEST)
    row_blocks = full_rows // block_size
    onehot = (block_rows[0][None, :] == jnp.arange(row_blocks, dtype=jnp.int32)[:, None]).astype(
        jnp.float32
    )
    partial_value = jnp.dot(
        onehot,
        products.reshape(block_count, block_size * num_cases),
        precision=lax.Precision.HIGHEST,
    )
    partial_value = partial_value.reshape(full_rows, num_cases)
    embedded = lax.dynamic_update_slice(
        jnp.zeros((full_rows, num_cases), jnp.float32), boundary, (position * quarter, 0)
    )
    contribution = embedded - partial_value
    current = lax.psum(contribution, "case")
    leaf_share = lax.dynamic_slice_in_dim(current, position * quarter, quarter, 0)
    slot = lax.axis_index("sub")
    levels = lax.axis_size("sub").bit_length() - 1
    nodes = jnp.zeros((quarter, num_cases), jnp.float32)
    for level in range(1, levels + 1):
        half = 1 << level - 1
        maps = interface_maps[0, level - 1]
        matrix = merge_maps[0, level - 1]
        shared_rows = matrix.shape[1]
        kept_index = jnp.concatenate([maps[0, shared_rows:], maps[1, shared_rows:] + full_rows])
        mine = lax.dynamic_slice_in_dim(kept_index, position * quarter, quarter)
        other = from_partner(current, "sub", level - 1)
        own_full, other_full = (current, other)
        upper = slot // half % 2 == 1
        left_full = jnp.where(upper, other_full, own_full)
        right_full = jnp.where(upper, own_full, other_full)
        stacked = jnp.concatenate([left_full, right_full], axis=0)
        shared = jnp.take(stacked, maps[0, :shared_rows], axis=0) + jnp.take(
            stacked, maps[1, :shared_rows] + full_rows, axis=0
        )
        parent = jnp.take(stacked, mine, axis=0) - jnp.dot(
            matrix, shared, precision=lax.Precision.HIGHEST
        )
        is_node = slot % (2 * half) == half
        if level == levels:
            is_node = jnp.logical_or(is_node, slot == 0)
        nodes = jnp.where(is_node, parent, nodes)
        if level < levels:
            current = lax.all_gather(parent, "case", axis=0, tiled=True)
    return (leaf_share[None], nodes[None])


def solution(mesh):
    placed = (
        P("sub", None, "case"),
        P("sub", None, "case"),
        P("sub", "case", None),
        P("sub", "case"),
        P("sub", "case"),
        P("sub", None, None, None),
        P("sub", None, "case", None),
    )
    return jax.shard_map(
        on_device,
        mesh=mesh,
        in_specs=placed,
        out_specs=(P("sub", "case", None), P("sub", "case", None)),
        check_vma=False,
    )
```

profile of v0, /device:TPU:8, one launch (start us, length us, event | category | flops | bytes accessed | tf_op | source)
XLA Modules:
  0.0 423.4 jit_solution(13161478264808261519)
XLA Ops:
  8.9 19.6 %all-to-all-start = ((f32[1,128,256]{2,0,1:T(1,128)}), f32[1,128,256]{2,0,1:T(1,128)S(1)}, u32[]{:S(2)}, u32[]{:S(2)}) async-start(f32[1,128,256]{2,0,1:T(1,128)} %copy.64), calls=%async_computation | async-start | bytes 262144 | tf_op jit(solution)/shard_map/all_to_all | solution.py:20
  28.5 2.4 copy.66
  32.8 12.9 %all-to-all-done = f32[1,128,256]{2,0,1:T(1,128)S(1)} async-done(((f32[1,128,256]{2,0,1:T(1,128)}), f32[1,128,256]{2,0,1:T(1,128)S(1)}, u32[]{:S(2)}, u32[]{:S(2)}) %all-to-all-start) | async-done | bytes 131104 | tf_op jit(solution)/shard_map/all_to_all | solution.py:20
  45.7 7.2 %all-to-all-start.1 = ((f32[1,128,1024]{2,0,1:T(1,128)}), f32[1,128,1024]{2,0,1:T(1,128)S(1)}, u32[]{:S(2)}, u32[]{:S(2)}) async-start(f32[1,128,1024]{2,0,1:T(1,128)} %copy.66), calls=%async_computation.1 | async-start | bytes 1048576 | tf_op jit(solution)/shard_map/all_to_all | solution.py:19
  55.1 31.4 %all-to-all-done.1 = f32[1,128,1024]{2,0,1:T(1,128)S(1)} async-done(((f32[1,128,1024]{2,0,1:T(1,128)}), f32[1,128,1024]{2,0,1:T(1,128)S(1)}, u32[]{:S(2)}, u32[]{:S(2)}) %all-to-all-start.1) | async-done | bytes 524320 | tf_op jit(solution)/shard_map/all_to_all | solution.py:19
  90.9 50.0 %all-reduce.2.cloned.1.call-done = f32[1024,128]{1,0:T(8,128)} async-done(((f32[1024,128]{1,0:T(8,128)}), f32[1024,128]{1,0:T(8,128)}) %all-reduce.2.cloned.1.call-update) | async-done | bytes 524304 | tf_op jit(solution)/shard_map/psum | solution.py:52
  140.8 1.9 collective-permute-start
  142.8 2.0 collective-permute-done
  149.0 1.9 fusion.8
  150.9 12.8 %all_gather.18 = f32[1024,128]{0,1:T(8,128)S(1)} all-gather(f32[256,128]{0,1:T(8,128)S(1)} %fusion.8), channel_id=1, replica_groups=mesh['sub'=128,'case'=4] {'case'}, dimensions={0}, use_global_device_ids=true | all-gather | bytes 655360 | tf_op jit(solution)/shard_map/all_gather | solution.py:81
  163.6 3.6 collective-permute-start.1
  167.4 9.3 %collective-permute-done.1 = f32[1024,128]{0,1:T(8,128)S(1)} collective-permute-done((f32[1024,128]{0,1:T(8,128)S(1)}, f32[1024,128]{0,1:T(8,128)S(1)}, u32[]{:S(2)}, u32[]{:S(2)}) %collective-permute-start.1) | collective-permute-done | bytes 524320 | tf_op jit(solution)/shard_map/ppermute | solution.py:12
  180.1 1.9 fusion.7
  182.0 13.1 %all_gather.19 = f32[1024,128]{0,1:T(8,128)S(1)} all-gather(f32[256,128]{0,1:T(8,128)S(1)} %fusion.7), channel_id=1, replica_groups=mesh['sub'=128,'case'=4] {'case'}, dimensions={0}, use_global_device_ids=true | all-gather | bytes 655360 | tf_op jit(solution)/shard_map/all_gather | solution.py:81
  195.1 4.4 %collective-permute-start.2 = (f32[1024,128]{0,1:T(8,128)S(1)}, f32[1024,128]{0,1:T(8,128)S(1)}, u32[]{:S(2)}, u32[]{:S(2)}) collective-permute-start(f32[1024,128]{0,1:T(8,128)S(1)} %all_gather.19), channel_id=1, source_target_pairs={{0,16},{4,20},{8,24},{12,28},{16,0},{20,4},{24,8},{28,12},{32,48},... | collective-permute-start | bytes 1572872 | tf_op jit(solution)/shard_map/ppermute | solution.py:12
  199.6 16.8 %collective-permute-done.2 = f32[1024,128]{0,1:T(8,128)S(1)} collective-permute-done((f32[1024,128]{0,1:T(8,128)S(1)}, f32[1024,128]{0,1:T(8,128)S(1)}, u32[]{:S(2)}, u32[]{:S(2)}) %collective-permute-start.2) | collective-permute-done | bytes 524320 | tf_op jit(solution)/shard_map/ppermute | solution.py:12
  219.9 1.9 fusion.6
  221.8 13.3 %all_gather.20 = f32[1024,128]{0,1:T(8,128)S(1)} all-gather(f32[256,128]{0,1:T(8,128)S(1)} %fusion.6), channel_id=1, replica_groups=mesh['sub'=128,'case'=4] {'case'}, dimensions={0}, use_global_device_ids=true | all-gather | bytes 655360 | tf_op jit(solution)/shard_map/all_gather | solution.py:81
  235.1 7.6 %collective-permute-start.3 = (f32[1024,128]{0,1:T(8,128)S(1)}, f32[1024,128]{0,1:T(8,128)S(1)}, u32[]{:S(2)}, u32[]{:S(2)}) collective-permute-start(f32[1024,128]{0,1:T(8,128)S(1)} %all_gather.20), channel_id=1, source_target_pairs={{0,32},{4,36},{8,40},{12,44},{16,48},{20,52},{24,56},{28,60},{32,0... | collective-permute-start | bytes 1572872 | tf_op jit(solution)/shard_map/ppermute | solution.py:12
  242.8 40.0 %collective-permute-done.3 = f32[1024,128]{0,1:T(8,128)S(1)} collective-permute-done((f32[1024,128]{0,1:T(8,128)S(1)}, f32[1024,128]{0,1:T(8,128)S(1)}, u32[]{:S(2)}, u32[]{:S(2)}) %collective-permute-start.3) | collective-permute-done | bytes 524320 | tf_op jit(solution)/shard_map/ppermute | solution.py:12
  286.2 1.9 fusion.5
  288.1 12.8 %all_gather.21 = f32[1024,128]{0,1:T(8,128)S(1)} all-gather(f32[256,128]{0,1:T(8,128)S(1)} %fusion.5), channel_id=1, replica_groups=mesh['sub'=128,'case'=4] {'case'}, dimensions={0}, use_global_device_ids=true | all-gather | bytes 655360 | tf_op jit(solution)/shard_map/all_gather | solution.py:81
  300.9 11.2 %collective-permute-start.4 = (f32[1024,128]{0,1:T(8,128)S(1)}, f32[1024,128]{0,1:T(8,128)S(1)}, u32[]{:S(2)}, u32[]{:S(2)}) collective-permute-start(f32[1024,128]{0,1:T(8,128)S(1)} %all_gather.21), channel_id=1, source_target_pairs={{0,64},{4,68},{8,72},{12,76},{16,80},{20,84},{24,88},{28,92},{32,9... | collective-permute-start | bytes 1572872 | tf_op jit(solution)/shard_map/ppermute | solution.py:12
  312.1 36.2 %collective-permute-done.4 = f32[1024,128]{0,1:T(8,128)S(1)} collective-permute-done((f32[1024,128]{0,1:T(8,128)S(1)}, f32[1024,128]{0,1:T(8,128)S(1)}, u32[]{:S(2)}, u32[]{:S(2)}) %collective-permute-start.4) | collective-permute-done | bytes 524320 | tf_op jit(solution)/shard_map/ppermute | solution.py:12
  351.7 1.9 fusion.4
  353.6 13.2 %all_gather.22 = f32[1024,128]{0,1:T(8,128)S(1)} all-gather(f32[256,128]{0,1:T(8,128)S(1)} %fusion.4), channel_id=1, replica_groups=mesh['sub'=128,'case'=4] {'case'}, dimensions={0}, use_global_device_ids=true | all-gather | bytes 655360 | tf_op jit(solution)/shard_map/all_gather | solution.py:81
  366.8 2.4 collective-permute-start.5
  369.3 10.0 %collective-permute-done.5 = f32[1024,128]{0,1:T(8,128)S(1)} collective-permute-done((f32[1024,128]{0,1:T(8,128)S(1)}, f32[1024,128]{0,1:T(8,128)S(1)}, u32[]{:S(2)}, u32[]{:S(2)}) %collective-permute-start.5) | collective-permute-done | bytes 524320 | tf_op jit(solution)/shard_map/ppermute | solution.py:12
  384.6 13.3 %all_gather.23 = f32[1024,128]{0,1:T(8,128)S(1)} all-gather(f32[256,128]{0,1:T(8,128)S(1)} %fusion.3), channel_id=1, replica_groups=mesh['sub'=128,'case'=4] {'case'}, dimensions={0}, use_global_device_ids=true | all-gather | bytes 655360 | tf_op jit(solution)/shard_map/all_gather | solution.py:81
  397.8 4.0 collective-permute-start.6
  403.5 6.9 %collective-permute-done.6 = f32[1024,128]{0,1:T(8,128)S(1)} collective-permute-done((f32[1024,128]{0,1:T(8,128)S(1)}, f32[1024,128]{0,1:T(8,128)S(1)}, u32[]{:S(2)}, u32[]{:S(2)}) %collective-permute-start.6) | collective-permute-done | bytes 524320 | tf_op jit(solution)/shard_map/ppermute | solution.py:12
  413.8 1.9 fusion.2
  (132 shorter events, 38.4 us)
Async XLA Ops:
  7.2 47.8 %copy-start.1 = (s32[1,32]{1,0:T(1,128)S(1)}, s32[1,32]{1,0:T(1,128)}, u32[]{:S(2)}) copy-start(s32[1,32]{1,0:T(1,128)} %param.15) | copy-start | bytes 388
  8.9 36.8 %all-to-all-start = ((f32[1,128,256]{2,0,1:T(1,128)}), f32[1,128,256]{2,0,1:T(1,128)S(1)}, u32[]{:S(2)}, u32[]{:S(2)}) async-start(f32[1,128,256]{2,0,1:T(1,128)} %copy.64), calls=%async_computation | async-start | bytes 262144 | tf_op jit(solution)/shard_map/all_to_all | solution.py:20
  45.7 40.8 %all-to-all-start.1 = ((f32[1,128,1024]{2,0,1:T(1,128)}), f32[1,128,1024]{2,0,1:T(1,128)S(1)}, u32[]{:S(2)}, u32[]{:S(2)}) async-start(f32[1,128,1024]{2,0,1:T(1,128)} %copy.66), calls=%async_computation.1 | async-start | bytes 1048576 | tf_op jit(solution)/shard_map/all_to_all | solution.py:19
  52.9 87.9 %all-reduce.2.cloned.1.call-start = ((), (), s32[]{:S(2)}) async-start(), calls=%async_computation.2 | async-start | bytes 1048576 | tf_op jit(solution)/shard_map/psum | solution.py:52
  54.9 33.8 %copy-start = (s32[1,32]{1,0:T(1,128)S(1)}, s32[1,32]{1,0:T(1,128)}, u32[]{:S(2)}) copy-start(s32[1,32]{1,0:T(1,128)} %param.14) | copy-start | bytes 388
  140.8 4.0 collective-permute-start
  163.6 13.0 %collective-permute-start.1 = (f32[1024,128]{0,1:T(8,128)S(1)}, f32[1024,128]{0,1:T(8,128)S(1)}, u32[]{:S(2)}, u32[]{:S(2)}) collective-permute-start(f32[1024,128]{0,1:T(8,128)S(1)} %all_gather.18), channel_id=1, source_target_pairs={{0,8},{4,12},{8,0},{12,4},{16,24},{20,28},{24,16},{28,20},{32,40},... | collective-permute-start | bytes 1572872 | tf_op jit(solution)/shard_map/ppermute | solution.py:12
  195.1 21.3 %collective-permute-start.2 = (f32[1024,128]{0,1:T(8,128)S(1)}, f32[1024,128]{0,1:T(8,128)S(1)}, u32[]{:S(2)}, u32[]{:S(2)}) collective-permute-start(f32[1024,128]{0,1:T(8,128)S(1)} %all_gather.19), channel_id=1, source_target_pairs={{0,16},{4,20},{8,24},{12,28},{16,0},{20,4},{24,8},{28,12},{32,48},... | collective-permute-start | bytes 1572872 | tf_op jit(solution)/shard_map/ppermute | solution.py:12
  235.1 47.6 %collective-permute-start.3 = (f32[1024,128]{0,1:T(8,128)S(1)}, f32[1024,128]{0,1:T(8,128)S(1)}, u32[]{:S(2)}, u32[]{:S(2)}) collective-permute-start(f32[1024,128]{0,1:T(8,128)S(1)} %all_gather.20), channel_id=1, source_target_pairs={{0,32},{4,36},{8,40},{12,44},{16,48},{20,52},{24,56},{28,60},{32,0... | collective-permute-start | bytes 1572872 | tf_op jit(solution)/shard_map/ppermute | solution.py:12
  300.9 47.4 %collective-permute-start.4 = (f32[1024,128]{0,1:T(8,128)S(1)}, f32[1024,128]{0,1:T(8,128)S(1)}, u32[]{:S(2)}, u32[]{:S(2)}) collective-permute-start(f32[1024,128]{0,1:T(8,128)S(1)} %all_gather.21), channel_id=1, source_target_pairs={{0,64},{4,68},{8,72},{12,76},{16,80},{20,84},{24,88},{28,92},{32,9... | collective-permute-start | bytes 1572872 | tf_op jit(solution)/shard_map/ppermute | solution.py:12
  366.8 12.5 %collective-permute-start.5 = (f32[1024,128]{0,1:T(8,128)S(1)}, f32[1024,128]{0,1:T(8,128)S(1)}, u32[]{:S(2)}, u32[]{:S(2)}) collective-permute-start(f32[1024,128]{0,1:T(8,128)S(1)} %all_gather.22), channel_id=1, source_target_pairs={{0,128},{4,132},{8,136},{12,140},{16,144},{20,148},{24,152},{28,15... | collective-permute-start | bytes 1572872 | tf_op jit(solution)/shard_map/ppermute | solution.py:12
  397.8 12.6 %collective-permute-start.6 = (f32[1024,128]{0,1:T(8,128)S(1)}, f32[1024,128]{0,1:T(8,128)S(1)}, u32[]{:S(2)}, u32[]{:S(2)}) collective-permute-start(f32[1024,128]{0,1:T(8,128)S(1)} %all_gather.23), channel_id=1, source_target_pairs={{0,256},{4,260},{8,264},{12,268},{16,272},{20,276},{24,280},{28,28... | collective-permute-start | bytes 1572872 | tf_op jit(solution)/shard_map/ppermute | solution.py:12
Sparse Core Ops, SparseCore 0:
  91.0 49.8 all-reduce.1
where the time goes:
time: 424 us; the launch traced here: 423 us
  waiting for transfers between devices  215 us (51%)
  blocking collectives  78.5 us (19%)
  starting transfers between devices  62.1 us (15%)
  local copies, waits for them, and re-layouts  32.1 us (8%)
  matrix products  15.4 us (4%)
  between operations  15.3 us (4%)
  other arithmetic  4.42 us (1%)
    ppermute x7, waiting for transfers between devices, from_partner(): return lax.ppermute(value, axis, pairs)  121 us
    all_gather x6, blocking collectives, on_device(): current = lax.all_gather(parent, 'case', axis=0, tiled=True)  78.5 us
    psum x1, waiting for transfers between devices, on_device(): current = lax.psum(contribution, 'case')  50 us
    ppermute x7, starting transfers between devices, from_partner(): return lax.ppermute(value, axis, pairs)  35.3 us
    all_to_all x1, waiting for transfers between devices, on_device(): lax.all_to_all(load_interior, 'sub', split_axis=1, concat_axis=0, tiled=T...  31.4 us
    all_to_all x1, starting transfers between devices, on_device(): lax.all_to_all(load_boundary, 'sub', split_axis=1, concat_axis=0, tiled=T...  19.6 us
    dot_general x7, matrix products, on_device(): jnp.dot(matrix, shared, precision=lax.Precision.HIGHEST)  13.2 us
    all_to_all x1, waiting for transfers between devices, on_device(): lax.all_to_all(load_boundary, 'sub', split_axis=1, concat_axis=0, tiled=T...  12.9 us
  transfers between devices with their start and end apart: 10, of which 10 were waited for; matrix products, arithmetic and copies ran while one was open for 2% of the time, Pallas kernels for 0%

commit v1 on v0

--- a/solution.py
+++ b/solution.py
@@ -78,7 +78,8 @@
             is_node = jnp.logical_or(is_node, slot == 0)
         nodes = jnp.where(is_node, parent, nodes)
         if level < levels:
-            current = lax.all_gather(parent, "case", axis=0, tiled=True)
+            repeated = jnp.stack([parent] * lax.axis_size("case"))
+            current = jnp.concatenate(lax.all_to_all(repeated, "case", 0, 0), axis=0)
     return (leaf_share[None], nodes[None])
 
 

time: 424 us -> 439 us (1.035)
  blocking collectives: 78.5 us -> 0 us
  waiting for transfers between devices: 215 us -> 283 us
  starting transfers between devices: 62.1 us -> 83.4 us
    all_gather x6 -> x0, blocking collectives: 78.5 us -> none  [on_device(): current = lax.all_gather(parent, 'case', axis=0, tiled=True)]
    all_to_all x0 -> x6, waiting for transfers between devices: none -> 54.4 us  [on_device(): current = jnp.concatenate(lax.all_to_all(repeated, 'case', 0, 0), axis=0)]
    all_to_all x0 -> x6, starting transfers between devices: none -> 21 us  [on_device(): current = jnp.concatenate(lax.all_to_all(repeated, 'case', 0, 0), axis=0)]
    ppermute x7, waiting for transfers between devices: 121 us -> 134 us  [from_partner(): return lax.ppermute(value, axis, pairs)]
    another operation x0 -> x6, local copies, waits for them, and re-layouts: none -> 5.14 us  [on_device(): repeated = jnp.stack([parent] * lax.axis_size('case'))]
  transfers between devices with their start and end apart: 10 -> 16, of which waited for: 10 -> 16; matrix products, arithmetic and copies ran while one was open for 2% -> 2% of each run, Pallas kernels for 0% -> 0%
where the time goes in v1:
time: 439 us; the launch traced here: 437 us
  waiting for transfers between devices  283 us (64%)
  starting transfers between devices  83.4 us (19%)
  local copies, waits for them, and re-layouts  35.9 us (8%)
  matrix products  15.4 us (4%)
  between operations  15.3 us (3%)
    ppermute x7, waiting for transfers between devices, from_partner(): return lax.ppermute(value, axis, pairs)  134 us
    all_to_all x6, waiting for transfers between devices, on_device(): current = jnp.concatenate(lax.all_to_all(repeated, 'case', 0, 0), axis=0)  54.4 us
    psum x1, waiting for transfers between devices, on_device(): current = lax.psum(contribution, 'case')  50 us
    ppermute x7, starting transfers between devices, from_partner(): return lax.ppermute(value, axis, pairs)  35.5 us
    all_to_all x1, waiting for transfers between devices, on_device(): lax.all_to_all(load_interior, 'sub', split_axis=1, concat_axis=0, tiled=T...  33.2 us
    all_to_all x6, starting transfers between devices, on_device(): current = jnp.concatenate(lax.all_to_all(repeated, 'case', 0, 0), axis=0)  21 us
    all_to_all x1, starting transfers between devices, on_device(): lax.all_to_all(load_boundary, 'sub', split_axis=1, concat_axis=0, tiled=T...  19.6 us
    dot_general x7, matrix products, on_device(): jnp.dot(matrix, shared, precision=lax.Precision.HIGHEST)  13.2 us
  transfers between devices with their start and end apart: 16, of which 16 were waited for; matrix products, arithmetic and copies ran while one was open for 2% of the time, Pallas kernels for 0%

profile of v1, /device:TPU:8, one launch (start us, length us, event | category | flops | bytes accessed | tf_op | source)
XLA Modules:
  0.0 437.3 jit_solution(12870179634023051125)
XLA Ops:
  8.9 19.6 %all-to-all-start = ((f32[1,128,256]{2,0,1:T(1,128)}), f32[1,128,256]{2,0,1:T(1,128)S(1)}, u32[]{:S(2)}, u32[]{:S(2)}) async-start(f32[1,128,256]{2,0,1:T(1,128)} %copy.40), calls=%async_computation | async-start | bytes 262144 | tf_op jit(solution)/shard_map/all_to_all | solution.py:20
  30.1 2.4 copy.42
  34.1 11.6 %all-to-all-done = f32[1,128,256]{2,0,1:T(1,128)S(1)} async-done(((f32[1,128,256]{2,0,1:T(1,128)}), f32[1,128,256]{2,0,1:T(1,128)S(1)}, u32[]{:S(2)}, u32[]{:S(2)}) %all-to-all-start) | async-done | bytes 131104 | tf_op jit(solution)/shard_map/all_to_all | solution.py:20
  45.7 7.2 %all-to-all-start.1 = ((f32[1,128,1024]{2,0,1:T(1,128)}), f32[1,128,1024]{2,0,1:T(1,128)S(1)}, u32[]{:S(2)}, u32[]{:S(2)}) async-start(f32[1,128,1024]{2,0,1:T(1,128)} %copy.42), calls=%async_computation.1 | async-start | bytes 1048576 | tf_op jit(solution)/shard_map/all_to_all | solution.py:19
  53.4 33.2 %all-to-all-done.1 = f32[1,128,1024]{2,0,1:T(1,128)S(1)} async-done(((f32[1,128,1024]{2,0,1:T(1,128)}), f32[1,128,1024]{2,0,1:T(1,128)S(1)}, u32[]{:S(2)}, u32[]{:S(2)}) %all-to-all-start.1) | async-done | bytes 524320 | tf_op jit(solution)/shard_map/all_to_all | solution.py:19
  90.9 50.0 %all-reduce.2.cloned.1.call-done = f32[1024,128]{1,0:T(8,128)} async-done(((f32[1024,128]{1,0:T(8,128)}), f32[1024,128]{1,0:T(8,128)}) %all-reduce.2.cloned.1.call-update) | async-done | bytes 524304 | tf_op jit(solution)/shard_map/psum | solution.py:52
  140.9 1.9 collective-permute-start
  142.8 2.0 collective-permute-done
  151.8 3.6 all-to-all-start.2
  155.5 9.8 %all-to-all-done.2 = f32[4,256,128]{2,1,0:T(8,128)S(1)} async-done(((f32[4,256,128]{2,1,0:T(8,128)}), f32[4,256,128]{2,1,0:T(8,128)S(1)}, u32[]{:S(2)}, u32[]{:S(2)}) %all-to-all-start.2) | async-done | bytes 524320 | tf_op jit(solution)/shard_map/all_to_all | solution.py:82
  165.3 3.6 collective-permute-start.1
  169.0 11.1 %collective-permute-done.1 = f32[1024,128]{1,0:T(8,128)S(1)} collective-permute-done((f32[1024,128]{1,0:T(8,128)S(1)}, f32[1024,128]{1,0:T(8,128)S(1)}, u32[]{:S(2)}, u32[]{:S(2)}) %collective-permute-start.1) | collective-permute-done | bytes 524320 | tf_op jit(solution)/shard_map/ppermute | solution.py:12
  186.0 3.5 all-to-all-start.3
  189.5 8.0 %all-to-all-done.3 = f32[4,256,128]{2,1,0:T(8,128)S(1)} async-done(((f32[4,256,128]{2,1,0:T(8,128)}), f32[4,256,128]{2,1,0:T(8,128)S(1)}, u32[]{:S(2)}, u32[]{:S(2)}) %all-to-all-start.3) | async-done | bytes 524320 | tf_op jit(solution)/shard_map/all_to_all | solution.py:82
  197.5 4.5 %collective-permute-start.2 = (f32[1024,128]{1,0:T(8,128)S(1)}, f32[1024,128]{1,0:T(8,128)S(1)}, u32[]{:S(2)}, u32[]{:S(2)}) collective-permute-start(f32[1024,128]{1,0:T(8,128)S(1)} %bitcast.142), channel_id=1, source_target_pairs={{0,16},{4,20},{8,24},{12,28},{16,0},{20,4},{24,8},{28,12},{32,48},... | collective-permute-start | bytes 1572872 | tf_op jit(solution)/shard_map/ppermute | solution.py:12
  202.1 20.3 %collective-permute-done.2 = f32[1024,128]{1,0:T(8,128)S(1)} collective-permute-done((f32[1024,128]{1,0:T(8,128)S(1)}, f32[1024,128]{1,0:T(8,128)S(1)}, u32[]{:S(2)}, u32[]{:S(2)}) %collective-permute-start.2) | collective-permute-done | bytes 524320 | tf_op jit(solution)/shard_map/ppermute | solution.py:12
  228.3 3.5 all-to-all-start.4
  231.8 8.8 %all-to-all-done.4 = f32[4,256,128]{2,1,0:T(8,128)S(1)} async-done(((f32[4,256,128]{2,1,0:T(8,128)}), f32[4,256,128]{2,1,0:T(8,128)S(1)}, u32[]{:S(2)}, u32[]{:S(2)}) %all-to-all-start.4) | async-done | bytes 524320 | tf_op jit(solution)/shard_map/all_to_all | solution.py:82
  240.6 7.6 %collective-permute-start.3 = (f32[1024,128]{1,0:T(8,128)S(1)}, f32[1024,128]{1,0:T(8,128)S(1)}, u32[]{:S(2)}, u32[]{:S(2)}) collective-permute-start(f32[1024,128]{1,0:T(8,128)S(1)} %bitcast.146), channel_id=1, source_target_pairs={{0,32},{4,36},{8,40},{12,44},{16,48},{20,52},{24,56},{28,60},{32,0... | collective-permute-start | bytes 1572872 | tf_op jit(solution)/shard_map/ppermute | solution.py:12
  248.4 42.4 %collective-permute-done.3 = f32[1024,128]{1,0:T(8,128)S(1)} collective-permute-done((f32[1024,128]{1,0:T(8,128)S(1)}, f32[1024,128]{1,0:T(8,128)S(1)}, u32[]{:S(2)}, u32[]{:S(2)}) %collective-permute-start.3) | collective-permute-done | bytes 524320 | tf_op jit(solution)/shard_map/ppermute | solution.py:12
  296.7 3.5 all-to-all-start.5
  300.2 9.9 %all-to-all-done.5 = f32[4,256,128]{2,1,0:T(8,128)S(1)} async-done(((f32[4,256,128]{2,1,0:T(8,128)}), f32[4,256,128]{2,1,0:T(8,128)S(1)}, u32[]{:S(2)}, u32[]{:S(2)}) %all-to-all-start.5) | async-done | bytes 524320 | tf_op jit(solution)/shard_map/all_to_all | solution.py:82
  310.1 11.5 %collective-permute-start.4 = (f32[1024,128]{1,0:T(8,128)S(1)}, f32[1024,128]{1,0:T(8,128)S(1)}, u32[]{:S(2)}, u32[]{:S(2)}) collective-permute-start(f32[1024,128]{1,0:T(8,128)S(1)} %bitcast.144), channel_id=1, source_target_pairs={{0,64},{4,68},{8,72},{12,76},{16,80},{20,84},{24,88},{28,92},{32,9... | collective-permute-start | bytes 1572872 | tf_op jit(solution)/shard_map/ppermute | solution.py:12
  321.7 37.1 %collective-permute-done.4 = f32[1024,128]{1,0:T(8,128)S(1)} collective-permute-done((f32[1024,128]{1,0:T(8,128)S(1)}, f32[1024,128]{1,0:T(8,128)S(1)}, u32[]{:S(2)}, u32[]{:S(2)}) %collective-permute-start.4) | collective-permute-done | bytes 524320 | tf_op jit(solution)/shard_map/ppermute | solution.py:12
  364.7 3.5 all-to-all-start.6
  368.2 9.9 %all-to-all-done.6 = f32[4,256,128]{2,1,0:T(8,128)S(1)} async-done(((f32[4,256,128]{2,1,0:T(8,128)}), f32[4,256,128]{2,1,0:T(8,128)S(1)}, u32[]{:S(2)}, u32[]{:S(2)}) %all-to-all-start.6) | async-done | bytes 524320 | tf_op jit(solution)/shard_map/all_to_all | solution.py:82
  378.1 2.4 collective-permute-start.5
  380.6 12.4 %collective-permute-done.5 = f32[1024,128]{1,0:T(8,128)S(1)} collective-permute-done((f32[1024,128]{1,0:T(8,128)S(1)}, f32[1024,128]{1,0:T(8,128)S(1)}, u32[]{:S(2)}, u32[]{:S(2)}) %collective-permute-start.5) | collective-permute-done | bytes 524320 | tf_op jit(solution)/shard_map/ppermute | solution.py:12
  398.9 3.5 all-to-all-start.7
  402.5 8.0 %all-to-all-done.7 = f32[4,256,128]{2,1,0:T(8,128)S(1)} async-done(((f32[4,256,128]{2,1,0:T(8,128)}), f32[4,256,128]{2,1,0:T(8,128)S(1)}, u32[]{:S(2)}, u32[]{:S(2)}) %all-to-all-start.7) | async-done | bytes 524320 | tf_op jit(solution)/shard_map/all_to_all | solution.py:82
  410.5 3.9 collective-permute-start.6
  416.0 8.7 %collective-permute-done.6 = f32[1024,128]{1,0:T(8,128)S(1)} collective-permute-done((f32[1024,128]{1,0:T(8,128)S(1)}, f32[1024,128]{1,0:T(8,128)S(1)}, u32[]{:S(2)}, u32[]{:S(2)}) %collective-permute-start.6) | collective-permute-done | bytes 524320 | tf_op jit(solution)/shard_map/ppermute | solution.py:12
  (144 shorter events, 53.3 us)
Async XLA Ops:
  7.2 46.0 %copy-start.1 = (s32[1,32]{1,0:T(1,128)S(1)}, s32[1,32]{1,0:T(1,128)}, u32[]{:S(2)}) copy-start(s32[1,32]{1,0:T(1,128)} %param.15) | copy-start | bytes 388
  8.9 36.8 %all-to-all-start = ((f32[1,128,256]{2,0,1:T(1,128)}), f32[1,128,256]{2,0,1:T(1,128)S(1)}, u32[]{:S(2)}, u32[]{:S(2)}) async-start(f32[1,128,256]{2,0,1:T(1,128)} %copy.40), calls=%async_computation | async-start | bytes 262144 | tf_op jit(solution)/shard_map/all_to_all | solution.py:20
  45.7 40.9 %all-to-all-start.1 = ((f32[1,128,1024]{2,0,1:T(1,128)}), f32[1,128,1024]{2,0,1:T(1,128)S(1)}, u32[]{:S(2)}, u32[]{:S(2)}) async-start(f32[1,128,1024]{2,0,1:T(1,128)} %copy.42), calls=%async_computation.1 | async-start | bytes 1048576 | tf_op jit(solution)/shard_map/all_to_all | solution.py:19
  52.9 87.9 %all-reduce.2.cloned.1.call-start = ((), (), s32[]{:S(2)}) async-start(), calls=%async_computation.8 | async-start | bytes 1048576 | tf_op jit(solution)/shard_map/psum | solution.py:52
  53.2 35.6 %copy-start = (s32[1,32]{1,0:T(1,128)S(1)}, s32[1,32]{1,0:T(1,128)}, u32[]{:S(2)}) copy-start(s32[1,32]{1,0:T(1,128)} %param.14) | copy-start | bytes 388
  140.9 4.0 collective-permute-start
  151.8 13.5 %all-to-all-start.2 = ((f32[4,256,128]{2,1,0:T(8,128)}), f32[4,256,128]{2,1,0:T(8,128)S(1)}, u32[]{:S(2)}, u32[]{:S(2)}) async-start(f32[4,256,128]{2,1,0:T(8,128)} %stack.12), calls=%async_computation.2 | async-start | bytes 1048576 | tf_op jit(solution)/shard_map/all_to_all | solution.py:82
  165.3 14.8 %collective-permute-start.1 = (f32[1024,128]{1,0:T(8,128)S(1)}, f32[1024,128]{1,0:T(8,128)S(1)}, u32[]{:S(2)}, u32[]{:S(2)}) collective-permute-start(f32[1024,128]{1,0:T(8,128)S(1)} %bitcast.145), channel_id=1, source_target_pairs={{0,8},{4,12},{8,0},{12,4},{16,24},{20,28},{24,16},{28,20},{32,40},... | collective-permute-start | bytes 1572872 | tf_op jit(solution)/shard_map/ppermute | solution.py:12
  186.0 11.5 %all-to-all-start.3 = ((f32[4,256,128]{2,1,0:T(8,128)}), f32[4,256,128]{2,1,0:T(8,128)S(1)}, u32[]{:S(2)}, u32[]{:S(2)}) async-start(f32[4,256,128]{2,1,0:T(8,128)} %stack.13), calls=%async_computation.3 | async-start | bytes 1048576 | tf_op jit(solution)/shard_map/all_to_all | solution.py:82
  197.5 24.9 %collective-permute-start.2 = (f32[1024,128]{1,0:T(8,128)S(1)}, f32[1024,128]{1,0:T(8,128)S(1)}, u32[]{:S(2)}, u32[]{:S(2)}) collective-permute-start(f32[1024,128]{1,0:T(8,128)S(1)} %bitcast.142), channel_id=1, source_target_pairs={{0,16},{4,20},{8,24},{12,28},{16,0},{20,4},{24,8},{28,12},{32,48},... | collective-permute-start | bytes 1572872 | tf_op jit(solution)/shard_map/ppermute | solution.py:12
  228.3 12.3 %all-to-all-start.4 = ((f32[4,256,128]{2,1,0:T(8,128)}), f32[4,256,128]{2,1,0:T(8,128)S(1)}, u32[]{:S(2)}, u32[]{:S(2)}) async-start(f32[4,256,128]{2,1,0:T(8,128)} %stack.14), calls=%async_computation.4 | async-start | bytes 1048576 | tf_op jit(solution)/shard_map/all_to_all | solution.py:82
  240.6 50.1 %collective-permute-start.3 = (f32[1024,128]{1,0:T(8,128)S(1)}, f32[1024,128]{1,0:T(8,128)S(1)}, u32[]{:S(2)}, u32[]{:S(2)}) collective-permute-start(f32[1024,128]{1,0:T(8,128)S(1)} %bitcast.146), channel_id=1, source_target_pairs={{0,32},{4,36},{8,40},{12,44},{16,48},{20,52},{24,56},{28,60},{32,0... | collective-permute-start | bytes 1572872 | tf_op jit(solution)/shard_map/ppermute | solution.py:12
  296.7 13.4 %all-to-all-start.5 = ((f32[4,256,128]{2,1,0:T(8,128)}), f32[4,256,128]{2,1,0:T(8,128)S(1)}, u32[]{:S(2)}, u32[]{:S(2)}) async-start(f32[4,256,128]{2,1,0:T(8,128)} %stack.15), calls=%async_computation.5 | async-start | bytes 1048576 | tf_op jit(solution)/shard_map/all_to_all | solution.py:82
  310.1 48.7 %collective-permute-start.4 = (f32[1024,128]{1,0:T(8,128)S(1)}, f32[1024,128]{1,0:T(8,128)S(1)}, u32[]{:S(2)}, u32[]{:S(2)}) collective-permute-start(f32[1024,128]{1,0:T(8,128)S(1)} %bitcast.144), channel_id=1, source_target_pairs={{0,64},{4,68},{8,72},{12,76},{16,80},{20,84},{24,88},{28,92},{32,9... | collective-permute-start | bytes 1572872 | tf_op jit(solution)/shard_map/ppermute | solution.py:12
  364.7 13.4 %all-to-all-start.6 = ((f32[4,256,128]{2,1,0:T(8,128)}), f32[4,256,128]{2,1,0:T(8,128)S(1)}, u32[]{:S(2)}, u32[]{:S(2)}) async-start(f32[4,256,128]{2,1,0:T(8,128)} %stack.16), calls=%async_computation.6 | async-start | bytes 1048576 | tf_op jit(solution)/shard_map/all_to_all | solution.py:82
  378.1 14.9 %collective-permute-start.5 = (f32[1024,128]{1,0:T(8,128)S(1)}, f32[1024,128]{1,0:T(8,128)S(1)}, u32[]{:S(2)}, u32[]{:S(2)}) collective-permute-start(f32[1024,128]{1,0:T(8,128)S(1)} %bitcast.143), channel_id=1, source_target_pairs={{0,128},{4,132},{8,136},{12,140},{16,144},{20,148},{24,152},{28,15... | collective-permute-start | bytes 1572872 | tf_op jit(solution)/shard_map/ppermute | solution.py:12
  398.9 11.6 %all-to-all-start.7 = ((f32[4,256,128]{2,1,0:T(8,128)}), f32[4,256,128]{2,1,0:T(8,128)S(1)}, u32[]{:S(2)}, u32[]{:S(2)}) async-start(f32[4,256,128]{2,1,0:T(8,128)} %stack.17), calls=%async_computation.7 | async-start | bytes 1048576 | tf_op jit(solution)/shard_map/all_to_all | solution.py:82
  410.5 14.3 %collective-permute-start.6 = (f32[1024,128]{1,0:T(8,128)S(1)}, f32[1024,128]{1,0:T(8,128)S(1)}, u32[]{:S(2)}, u32[]{:S(2)}) collective-permute-start(f32[1024,128]{1,0:T(8,128)S(1)} %bitcast.141), channel_id=1, source_target_pairs={{0,256},{4,260},{8,264},{12,268},{16,272},{20,276},{24,280},{28,28... | collective-permute-start | bytes 1572872 | tf_op jit(solution)/shard_map/ppermute | solution.py:12
Sparse Core Ops, SparseCore 0:
  91.0 49.8 all-reduce.1
